TPU v7x, 128 devices: a whole 4x4x4 slice. The times are simulated.
128 devices in a mesh: seq: 32 (over x, y, core), fsdp: 4 (over z).
Axes of the slice: x: 4, y: 4, z: 4, core: 2. Of those that a mesh axis runs over, the one named last changes fastest.
Arguments:
- patches: bfloat16 [32768, 1280], P(('seq', 'fsdp')), may hold values from -6 to 6
- vis_index: int32 [32768], P(('seq', 'fsdp')), may hold values from 0 to 131071, as said below
- kv_list: int32 [256, 16], P(('seq', 'fsdp')), may hold values from 0 to 255, as said below
- kv_count: int32 [256], P(('seq', 'fsdp')), may hold values from 1 to 16, as said below
- global_tiles: int32 [2], replicated, may hold values from 0 to 255
- frame_table: bfloat16 [256, 1280], replicated, may hold values from -3 to 3
- space_table: bfloat16 [512, 1280], replicated, may hold values from -3 to 3
- ln_gain: bfloat16 [1280], replicated, may hold values from 0.25 to 1.75
- ln_bias: bfloat16 [1280], replicated, may hold values from -3 to 3
- w_qkv: bfloat16 [1280, 3840], P('fsdp')
- w_out: bfloat16 [1280, 1280], P('fsdp'), may hold values from -1.25 to 1.25
Outputs:
- attended: bfloat16 [32768, 1280], P(('seq', 'fsdp'))
Inputs may be any that keep to these rules, and one draw needn't show every extreme that they name: `vis_index`: exactly one visible position in each aligned group of four; strictly increasing. `kv_list`: the first entry of query tile i is i itself; entries may repeat; every entry t satisfies |t // 8 - i // 8| <= 2. Over all entries of an aligned run of 2 query tiles, the tiles that lie in any one group other than the run's own group (group = tile // 8) number at most 3 distinct ones, and exactly 3 for every such group within two of the run's own. On every device at least one query tile has kv_count = 16.
All inputs are finite; a program needn't handle non-finite values.
Results may differ from a plain program's by a relative error of at most 0.0065.
Values may be sent and summed in bfloat16 or wider, within the bound.
No kernel may reach another device: no remote copies, remote signals or barrier semaphores. Data moves between devices by JAX's collectives and lax.ppermute only.
A program may use at most 192 MiB of HBM per device.

v0:
```python
import jax
import jax.numpy as jnp
from jax import lax
from jax.sharding import PartitionSpec as P

HEADS = 16
TILE = 128
KT = 16
GLOBAL = 2
PATCHES = 512
NEAR = 3
REACH = (-2, -1, 1, 2)


def passed_along(block, axis, distance):
    devices = range(lax.axis_size(axis))
    route = [(i - distance, i) for i in devices if i - distance in devices]
    return lax.ppermute(block, axis, route)


def layer_norm(stream, ln_gain, ln_bias):
    stream32 = stream.astype(jnp.float32)
    mean_val = jnp.mean(stream32, axis=-1, keepdims=True)
    centred = stream32 - mean_val
    variance = jnp.mean(centred * centred, axis=-1, keepdims=True)
    scaled = centred * lax.rsqrt(variance + 1e-06)
    return (scaled * ln_gain.astype(jnp.float32) + ln_bias.astype(jnp.float32)).astype(jnp.bfloat16)


def embed(patches, vis_index, frame_table, space_table):
    frame_ids = vis_index // PATCHES
    patch_ids = vis_index % PATCHES
    return (
        patches.astype(jnp.float32)
        + frame_table[frame_ids].astype(jnp.float32)
        + space_table[patch_ids].astype(jnp.float32)
    ).astype(jnp.bfloat16)


def near_tiles(entries, group, group_tiles):
    cand = group * group_tiles + jnp.arange(group_tiles, dtype=jnp.int32)
    named = jnp.any(entries.reshape(-1, 1) == cand[None, :], axis=0)
    rank = jnp.cumsum(named.astype(jnp.int32)) - 1
    local_ids = jnp.arange(group_tiles, dtype=jnp.int32)
    picks = jnp.stack([jnp.sum(jnp.where(named & (rank == j), local_ids, 0)) for j in range(NEAR)])
    return (picks, rank)


def attend_tile(query_tile, key_values, key_live, feat_width):
    head_size = feat_width // HEADS
    key_rows = key_values.shape[0]
    queries_h = query_tile.reshape(TILE, HEADS, head_size)
    keys_h = key_values[:, :feat_width].reshape(key_rows, HEADS, head_size)
    values_h = key_values[:, feat_width:].reshape(key_rows, HEADS, head_size)
    scores = jnp.einsum(
        "qhd,khd->hqk", queries_h, keys_h, preferred_element_type=jnp.float32
    ) * head_size ** (-0.5)
    scores = jnp.where(key_live[None, None, :], scores, -jnp.inf)
    row_max = jnp.max(scores, axis=-1, keepdims=True)
    weights_raw = jnp.exp(scores - row_max)
    probs = (weights_raw / jnp.sum(weights_raw, axis=-1, keepdims=True)).astype(jnp.bfloat16)
    mixed_h = jnp.einsum("hqk,khd->qhd", probs, values_h, preferred_element_type=jnp.float32)
    return mixed_h.reshape(TILE, feat_width).astype(jnp.bfloat16)


def local(
    patches,
    vis_index,
    kv_list,
    kv_count,
    global_tiles,
    frame_table,
    space_table,
    ln_gain,
    ln_bias,
    w_qkv,
    w_out,
):
    tok_rows = patches.shape[0]
    feat_width = patches.shape[1]
    tile_count = tok_rows // TILE
    fsdp_size = lax.axis_size("fsdp")
    seq_size = lax.axis_size("seq")
    seq_at = lax.axis_index("seq")
    dev_at = seq_at * fsdp_size + lax.axis_index("fsdp")
    group_tiles = tile_count * fsdp_size
    stream = embed(patches, vis_index, frame_table, space_table)
    global_rows = []
    for slot_no in range(GLOBAL):
        tile_id = global_tiles[slot_no]
        mine = tile_id // tile_count == dev_at
        rows = lax.dynamic_slice_in_dim(stream, tile_id % tile_count * TILE, TILE, 0)
        global_rows.append(jnp.where(mine, rows, jnp.zeros_like(rows)))
    global_stream = lax.psum(jnp.concatenate(global_rows, axis=0), ("seq", "fsdp"))
    w_full = lax.all_gather(w_qkv, "fsdp", axis=0, tiled=True)
    normed = layer_norm(stream, ln_gain, ln_bias)
    qkv = jnp.dot(normed, w_full, preferred_element_type=jnp.float32).astype(jnp.bfloat16)
    query = qkv[:, :feat_width]
    keyval = qkv[:, feat_width:]
    global_normed = layer_norm(global_stream, ln_gain, ln_bias)
    global_kv = (
        jnp.dot(global_normed, w_full[:, feat_width:], preferred_element_type=jnp.float32)
        .astype(jnp.bfloat16)
        .reshape(GLOBAL, TILE, 2 * feat_width)
    )
    group_block = lax.all_gather(keyval, "fsdp", axis=0, tiled=True).reshape(
        group_tiles, TILE, 2 * feat_width
    )
    seq_lists = lax.all_gather(kv_list, "seq", axis=0, tiled=True)
    near_blocks = []
    near_rank = []
    for reach in REACH:
        distance = -reach
        dest = jnp.clip(seq_at + distance, 0, seq_size - 1)
        dest_lists = lax.dynamic_slice_in_dim(seq_lists, dest * tile_count, tile_count, 0)
        send_ids, unused = near_tiles(dest_lists, seq_at, group_tiles)
        sent = passed_along(group_block[send_ids], "seq", distance)
        near_blocks.append(sent)
        unused2, rank = near_tiles(kv_list, seq_at + reach, group_tiles)
        near_rank.append(rank)
    window = jnp.concatenate([group_block] + near_blocks + [global_kv], axis=0)
    near_rank = jnp.stack(near_rank)
    entry_group = kv_list // group_tiles
    entry_local = kv_list % group_tiles
    reach_of = entry_group - seq_at
    reach_slot = jnp.where(reach_of < 0, reach_of + 2, reach_of + 1)
    reach_slot = jnp.clip(reach_slot, 0, len(REACH) - 1)
    entry_rank = near_rank[reach_slot, entry_local]
    local_lists = jnp.where(
        reach_of == 0, entry_local, group_tiles + NEAR * reach_slot + entry_rank
    )
    global_slots = group_tiles + NEAR * len(REACH) + jnp.arange(GLOBAL, dtype=jnp.int32)
    query_tiles = query.reshape(tile_count, TILE, feat_width)

    def per_tile(tile_args):
        query_tile, local_ids, live_count = tile_args
        slot_live_row = jnp.concatenate(
            [jnp.arange(KT) < live_count, jnp.ones((GLOBAL,), dtype=bool)]
        )
        key_live = jnp.repeat(slot_live_row, TILE)
        key_values = window[jnp.concatenate([local_ids, global_slots])].reshape(
            (KT + GLOBAL) * TILE, 2 * feat_width
        )
        return attend_tile(query_tile, key_values, key_live, feat_width)

    heads_out = lax.map(per_tile, (query_tiles, local_lists, kv_count)).reshape(
        tok_rows, feat_width
    )
    return jnp.dot(
        heads_out,
        lax.all_gather(w_out, "fsdp", axis=0, tiled=True),
        preferred_element_type=jnp.float32,
    ).astype(jnp.bfloat16)


def solution(mesh):
    return jax.shard_map(
        local,
        mesh=mesh,
        in_specs=(
            P(("seq", "fsdp"), None),
            P(("seq", "fsdp")),
            P(("seq", "fsdp"), None),
            P(("seq", "fsdp")),
            P(),
            P(),
            P(),
            P(),
            P(),
            P("fsdp", None),
            P("fsdp", None),
        ),
        out_specs=P(("seq", "fsdp"), None),
        check_vma=False,
    )
```

profile of v0, /device:TPU:28, one launch (start us, length us, event | category | flops | bytes accessed | tf_op | source)
XLA Modules:
  0.0 548.4 jit_solution(2590682510310247328)
XLA Ops:
  7.4 0.7 all-gather.5.cloned.1.call-update
  8.1 0.7 convert_element_type.181
  8.8 0.7 convert_element_type.182
  9.5 0.7 compare_select_fusion.2
  10.2 1.3 gather_fusion.2
  11.5 1.2 gather_fusion.3
  12.8 0.4 convert_reduce_fusion.1
  13.1 0.3 fusion.28
  13.5 93.8 %all-gather.5.cloned.1.call-done = bf16[1280,3840]{1,0:T(8,128)(2,1)} async-done(((bf16[320,3840]{1,0:T(8,128)(2,1)}), bf16[1280,3840]{1,0:T(8,128)(2,1)}) %all-gather.5.cloned.1.call-update) | async-done | bytes 9830416 | tf_op jit(solution)/shard_map/all_gather | solution.py:95
  107.2 6.6 %convolution_convert_fusion = bf16[256,3840]{1,0:T(8,128)(2,1)S(1)} fusion(bf16[1280,3840]{1,0:T(8,128)(2,1)} %all-gather.5.cloned.1.call-done, bf16[256,1280]{1,0:T(8,128)(2,1)S(1)} %get-tuple-element.114, f32[1280]{0:T(1024)S(1)} %convert_element_type.182, f32[1280]{0:T(1024)S(1)} %convert_element_type.181, f32[256]{0:T(256)S(1)} %add_rsqrt_fusion.1, ...), kind=kOutput, calls=%fused_computation.34 | convolution fusion | flops 2519531520 | bytes 12464128 | tf_op jit(solution)/shard_map/dot_general | solution.py:97
  113.9 1.2 copy-done.4
  115.2 1.2 slice.46
  116.4 0.6 fusion.80
  122.4 0.9 pad_maximum_fusion
  123.3 0.7 all-gather.9.cloned.1.call-update
  124.1 22.4 %all-gather = s32[32,2,16]{2,1,0:T(2,128)S(1)} all-gather(s32[1,2,16]{2,1,0:T(2,128)S(1)} %bitcast.181), channel_id=1, replica_groups=mesh['seq'=32,'fsdp'=4] {'seq'}, dimensions={0}, use_global_device_ids=true | all-gather | bytes 4224 | tf_op jit(solution)/shard_map/all_gather | solution.py:109
  146.8 0.2 compare_reduce_fusion
  147.3 0.7 fusion.65
  148.2 0.7 fusion.68
  148.9 3.8 fusion.61
  152.9 0.7 fusion.71
  153.9 0.7 fusion.74
  154.6 3.8 fusion.63
  158.4 0.2 compare_reduce_fusion.7
  159.5 0.8 gather_fusion.1
  160.4 14.5 %all-gather.7.cloned.1.call-done = bf16[1024,2560]{1,0:T(8,128)(2,1)} async-done(((bf16[256,2560]{1,0:T(8,128)(2,1)}), bf16[1024,2560]{1,0:T(8,128)(2,1)}) %all-gather.7.cloned.1.call-update) | async-done | bytes 5242896 | tf_op jit(solution)/shard_map/all_gather | solution.py:106
  174.9 4.6 gather_fusion.4
  179.5 3.0 collective-permute-start
  182.5 137.3 %all-reduce.3.cloned.1.call-done = bf16[256,1280]{1,0:T(8,128)(2,1)} async-done(((bf16[256,1280]{1,0:T(8,128)(2,1)}), bf16[256,1280]{1,0:T(8,128)(2,1)}) %all-reduce.3.cloned.1.call-update) | async-done | bytes 655376 | tf_op jit(solution)/shard_map/psum | solution.py:94
  319.8 1.3 convert_reduce_fusion
  321.2 4.5 gather_fusion.5
  325.7 2.1 collective-permute-start.1
  327.8 0.3 fusion.24
  328.1 4.6 gather_fusion.6
  332.7 3.4 collective-permute-start.2
  336.2 4.7 gather_fusion.7
  340.9 2.6 collective-permute-start.3
  343.5 4.8 fusion.17
  348.4 0.3 constant_dynamic-update-slice_fusion.6
  348.7 1.7 constant_dynamic-update-slice_fusion.5
  350.4 1.6 collective-permute-done.1
  351.9 1.7 constant_dynamic-update-slice_fusion.4
  353.6 19.3 %collective-permute-done.2 = bf16[3,128,2560]{2,1,0:T(8,128)(2,1)} collective-permute-done((bf16[3,128,2560]{2,1,0:T(8,128)(2,1)}, bf16[3,128,2560]{2,1,0:T(8,128)(2,1)}, u32[]{:S(2)}, u32[]{:S(2)}) %collective-permute-start.2) | collective-permute-done | bytes 1966112 | tf_op jit(solution)/shard_map/ppermute | solution.py:18
  373.0 1.7 constant_dynamic-update-slice_fusion.3
  374.7 30.7 %collective-permute-done.3 = bf16[3,128,2560]{2,1,0:T(8,128)(2,1)S(1)} collective-permute-done((bf16[3,128,2560]{2,1,0:T(8,128)(2,1)}, bf16[3,128,2560]{2,1,0:T(8,128)(2,1)S(1)}, u32[]{:S(2)}, u32[]{:S(2)}) %collective-permute-start.3) | collective-permute-done | bytes 1966112 | tf_op jit(solution)/shard_map/ppermute | solution.py:18
  405.6 5.0 copy-done.2
  410.6 126.7 %while.11 = (s32[]{:T(128)}, bf16[2,128,1280]{2,1,0:T(8,128)(2,1)S(1)}, s32[2,16]{1,0:T(2,128)S(1)}, bf16[22,128,2560]{2,1,0:T(8,128)(2,1)}, s32[2]{0:T(128)S(1)...) while((s32[]{:T(128)}, bf16[2,128,1280]{2,1,0:T(8,128)(2,1)S(1)}, ...), condition=%wide.region_36.37_spmd.clone, body=%wide.region_33.36_spmd.clone.sunk | while | flops 1538428160 | bytes 123626584 | solution.py:146
  410.7 11.3 %gather_fusion = bf16[18,128,2560]{2,1,0:T(8,128)(2,1)} fusion(bf16[22,128,2560]{2,1,0:T(8,128)(2,1)} %get-tuple-element.205, s32[1024]{0:T(1024)S(1)} %pad_clamp_fusion.8), kind=kCustom, calls=%fused_computation.clone.clone.1 | custom fusion | bytes 23593032 | tf_op jit(solution)/shard_map/while/body/eval_jaxpr/gather | solution.py:141
  422.0 9.7 %fusion.102 = (bf16[2304,1280]{1,0:T(8,128)(2,1)}, bf16[2304,1280]{1,0:T(8,128)(2,1)}) fusion(bf16[2304,2560]{1,0:T(8,128)(2,1)} %bitcast.166), kind=kLoop, calls=%fused_computation.186.clone.1 | loop fusion | bytes 23592960 | tf_op jit(solution)/shard_map/while/body/eval_jaxpr/slice | solution.py:53
  431.7 8.9 %copy.38 = bf16[2304,1280]{0,1:T(8,128)(2,1)} copy(bf16[2304,1280]{1,0:T(8,128)(2,1)} %get-tuple-element.183) | data formatting | bytes 11796480 | tf_op jit(solution)/shard_map/while
  440.7 0.6 dynamic_slice.54
  441.3 0.6 iota_compare_fusion.2
  442.1 11.3 %fusion.103 = (f32[16,128]{1,0:T(8,128)S(1)}, f32[16,128,2304]{2,1,0:T(8,128)}) fusion(pred[2304]{0:T(1024)(128)(4,1)S(1)} %broadcast_bitcast_fusion.2, bf16[128,16,80]{0,2,1:T(8,128)(2,1)S(1)} %bitcast.176, bf16[2304,16,80]{0,2,1:T(8,128)(2,1)} %bitcast.167), kind=kOutput, calls=%fused_computation.187.clone.1 | convolution fusion | flops 773851392 | bytes 25110784 | tf_op jit(solution)/shard_map/while/body/eval_jaxpr/sub | solution.py:60
  453.4 8.9 %copy.36 = bf16[2304,1280]{0,1:T(8,128)(2,1)} copy(bf16[2304,1280]{1,0:T(8,128)(2,1)} %get-tuple-element.182) | data formatting | bytes 11796480 | tf_op jit(solution)/shard_map/while
  462.2 11.5 %fusion.104 = bf16[16,80,128]{2,1,0:T(8,128)(2,1)S(1)} fusion(bf16[2304,16,80]{0,2,1:T(8,128)(2,1)} %bitcast.168, f32[16,128,2304]{2,1,0:T(8,128)} %get-tuple-element.184, f32[16,128]{1,0:T(8,128)S(1)} %get-tuple-element.185), kind=kOutput, calls=%fused_computation.19.clone.1 | convolution fusion | flops 764575744 | bytes 25108480 | tf_op jit(solution)/shard_map/while/body/eval_jaxpr/hqk,khd->qhd/dot_general | solution.py:62
  474.1 11.3 %gather_fusion = bf16[18,128,2560]{2,1,0:T(8,128)(2,1)} fusion(bf16[22,128,2560]{2,1,0:T(8,128)(2,1)} %get-tuple-element.205, s32[1024]{0:T(1024)S(1)} %pad_clamp_fusion.8), kind=kCustom, calls=%fused_computation.clone.clone.1 | custom fusion | bytes 23593032 | tf_op jit(solution)/shard_map/while/body/eval_jaxpr/gather | solution.py:141
  485.4 9.7 %fusion.102 = (bf16[2304,1280]{1,0:T(8,128)(2,1)}, bf16[2304,1280]{1,0:T(8,128)(2,1)}) fusion(bf16[2304,2560]{1,0:T(8,128)(2,1)} %bitcast.166), kind=kLoop, calls=%fused_computation.186.clone.1 | loop fusion | bytes 23592960 | tf_op jit(solution)/shard_map/while/body/eval_jaxpr/slice | solution.py:53
  495.0 8.9 %copy.38 = bf16[2304,1280]{0,1:T(8,128)(2,1)} copy(bf16[2304,1280]{1,0:T(8,128)(2,1)} %get-tuple-element.183) | data formatting | bytes 11796480 | tf_op jit(solution)/shard_map/while
  504.1 0.6 dynamic_slice.54
  504.7 0.6 iota_compare_fusion.2
  505.5 11.3 %fusion.103 = (f32[16,128]{1,0:T(8,128)S(1)}, f32[16,128,2304]{2,1,0:T(8,128)}) fusion(pred[2304]{0:T(1024)(128)(4,1)S(1)} %broadcast_bitcast_fusion.2, bf16[128,16,80]{0,2,1:T(8,128)(2,1)S(1)} %bitcast.176, bf16[2304,16,80]{0,2,1:T(8,128)(2,1)} %bitcast.167), kind=kOutput, calls=%fused_computation.187.clone.1 | convolution fusion | flops 773851392 | bytes 25110784 | tf_op jit(solution)/shard_map/while/body/eval_jaxpr/sub | solution.py:60
  516.7 8.9 %copy.36 = bf16[2304,1280]{0,1:T(8,128)(2,1)} copy(bf16[2304,1280]{1,0:T(8,128)(2,1)} %get-tuple-element.182) | data formatting | bytes 11796480 | tf_op jit(solution)/shard_map/while
  525.6 11.5 %fusion.104 = bf16[16,80,128]{2,1,0:T(8,128)(2,1)S(1)} fusion(bf16[2304,16,80]{0,2,1:T(8,128)(2,1)} %bitcast.168, f32[16,128,2304]{2,1,0:T(8,128)} %get-tuple-element.184, f32[16,128]{1,0:T(8,128)S(1)} %get-tuple-element.185), kind=kOutput, calls=%fused_computation.19.clone.1 | convolution fusion | flops 764575744 | bytes 25108480 | tf_op jit(solution)/shard_map/while/body/eval_jaxpr/hqk,khd->qhd/dot_general | solution.py:62
  537.4 3.9 convolution_convert_fusion.1
  (100 shorter events, 4.1 us)
Async XLA Ops:
  7.4 4.1 copy-start
  7.4 2.8 copy-start.3
  7.4 99.9 %all-gather.5.cloned.1.call-start = ((), (), s32[]{:S(2)}) async-start(), calls=%async_computation | async-start | bytes 12288000 | tf_op jit(solution)/shard_map/all_gather | solution.py:95
  8.1 166.8 %all-gather.7.cloned.1.call-start = ((), (), s32[]{:S(2)}) async-start(), calls=%async_computation.1 | async-start | bytes 6553600 | tf_op jit(solution)/shard_map/all_gather | solution.py:106
  11.5 1.3 copy-start.6
  113.9 1.3 copy-start.4
  115.1 1.2 copy-start.8
  116.3 7.7 %copy-start.7 = (s32[2,16]{1,0:T(2,128)S(1)}, s32[2,16]{1,0:T(2,128)}, u32[]{:S(2)}) copy-start(s32[2,16]{1,0:T(2,128)} %param.15) | copy-start | bytes 388
  116.3 203.5 %all-reduce.3.cloned.1.call-start = ((), (), s32[]{:S(2)}) async-start(), calls=%async_computation.2 | async-start | bytes 1310720 | tf_op jit(solution)/shard_map/psum | solution.py:94
  123.3 414.2 %all-gather.9.cloned.1.call-start = ((), (), s32[]{:S(2)}) async-start(), calls=%async_computation.3 | async-start | bytes 4096000 | tf_op jit(solution)/shard_map/all_gather | solution.py:151
  179.5 169.2 %collective-permute-start = (bf16[3,128,2560]{2,1,0:T(8,128)(2,1)}, bf16[3,128,2560]{2,1,0:T(8,128)(2,1)}, u32[]{:S(2)}, u32[]{:S(2)}) collective-permute-start(bf16[3,128,2560]{2,1,0:T(8,128)(2,1)} %gather_fusion.4), channel_id=1, source_target_pairs={{0,8},{4,12},{8,16},{12,20},{16,24},{20,28},{24,32},{28,36},{32,40... | collective-permute-start | bytes 5898248 | tf_op jit(solution)/shard_map/ppermute | solution.py:18
  319.8 8.0 %copy-start.5 = (bf16[256,1280]{1,0:T(8,128)(2,1)S(1)}, bf16[256,1280]{1,0:T(8,128)(2,1)}, u32[]{:S(2)}) copy-start(bf16[256,1280]{1,0:T(8,128)(2,1)} %all-reduce.3.cloned.1.call-done) | copy-start | bytes 1966084
  325.7 26.3 %collective-permute-start.1 = (bf16[3,128,2560]{2,1,0:T(8,128)(2,1)}, bf16[3,128,2560]{2,1,0:T(8,128)(2,1)}, u32[]{:S(2)}, u32[]{:S(2)}) collective-permute-start(bf16[3,128,2560]{2,1,0:T(8,128)(2,1)} %gather_fusion.5), channel_id=1, source_target_pairs={{0,4},{4,8},{8,12},{12,16},{16,20},{20,24},{24,28},{28,32},{32,36}... | collective-permute-start | bytes 5898248 | tf_op jit(solution)/shard_map/ppermute | solution.py:18
  332.7 40.3 %collective-permute-start.2 = (bf16[3,128,2560]{2,1,0:T(8,128)(2,1)}, bf16[3,128,2560]{2,1,0:T(8,128)(2,1)}, u32[]{:S(2)}, u32[]{:S(2)}) collective-permute-start(bf16[3,128,2560]{2,1,0:T(8,128)(2,1)} %gather_fusion.6), channel_id=1, source_target_pairs={{4,0},{8,4},{12,8},{16,12},{20,16},{24,20},{28,24},{32,28},{36,32}... | collective-permute-start | bytes 5898248 | tf_op jit(solution)/shard_map/ppermute | solution.py:18
  336.2 12.2 %slice-start = ((s8[5242880]{0:T(1024)(128)(4,1)}), s8[1048576]{0:T(1024)(128)(4,1)S(1)}, s32[]{:S(2)}) async-start(s8[5242880]{0:T(1024)(128)(4,1)} %bitcast.173), calls=%async_computation.4 | async-start | bytes 2097152
  340.9 7.5 %slice-start.1 = ((s8[5242880]{0:T(1024)(128)(4,1)}), s8[4194304]{0:T(1024)(128)(4,1)S(1)}, s32[]{:S(2)}) async-start(s8[5242880]{0:T(1024)(128)(4,1)} %bitcast.173), calls=%async_computation.5 | async-start | bytes 8388608
  340.9 64.5 %collective-permute-start.3 = (bf16[3,128,2560]{2,1,0:T(8,128)(2,1)}, bf16[3,128,2560]{2,1,0:T(8,128)(2,1)S(1)}, u32[]{:S(2)}, u32[]{:S(2)}) collective-permute-start(bf16[3,128,2560]{2,1,0:T(8,128)(2,1)} %gather_fusion.7), channel_id=1, source_target_pairs={{8,0},{12,4},{16,8},{20,12},{24,16},{28,20},{32,24},{36,28},{40,32... | collective-permute-start | bytes 5898248 | tf_op jit(solution)/shard_map/ppermute | solution.py:18
  374.6 36.0 %slice-start.2 = ((bf16[256,3840]{1,0:T(8,128)(2,1)}), bf16[256,1280]{1,0:T(8,128)(2,1)S(1)}, s32[]{:S(2)}) async-start(bf16[256,3840]{1,0:T(8,128)(2,1)} %copy-done.4), calls=%async_computation.6 | async-start | bytes 1310720 | tf_op jit(solution)/shard_map/slice | solution.py:98
  374.6 36.0 %copy-start.9 = (s32[2]{0:T(128)S(1)}, s32[2]{0:T(128)}, u32[]{:S(2)}) copy-start(s32[2]{0:T(128)} %param.16) | copy-start | bytes 28
  405.6 5.0 copy-start.2
  537.4 3.9 copy-start.1
Sparse Core Ops, SparseCore 0:
  9.8 97.3 all-gather.4
  116.5 58.4 all-gather.6
  176.6 41.3 all-gather.8
Sparse Core Ops, SparseCore 1:
  123.3 196.4 all-reduce.2
where the time goes:
time: 550 us; the launch traced here: 548 us
  waiting for transfers between devices  299 us (54%)
  local copies, waits for them, and re-layouts  115 us (21%)
  matrix products  61 us (11%)
  blocking collectives  22.4 us (4%)
  between operations  20.2 us (4%)
  other arithmetic  19.5 us (4%)
  starting transfers between devices  11.3 us (2%)
    psum x1, waiting for transfers between devices, local(): lax.psum(jnp.concatenate(global_rows, axis=0), ('seq', 'fsdp'))  137 us
    all_gather x1, waiting for transfers between devices, local(): w_full = lax.all_gather(w_qkv, 'fsdp', axis=0, tiled=True)  93.8 us
    ppermute x4, waiting for transfers between devices, passed_along(): return lax.ppermute(block, axis, route)  51.6 us
    while x4, local copies, waits for them, and re-layouts  35.4 us
    dot_general x2, matrix products, attend_tile(): jnp.einsum('hqk,khd->qhd', probs, values_h, preferred_element_type=jnp.fl...  23.1 us
    sub x2, matrix products, attend_tile(): weights_raw = jnp.exp(scores - row_max)  22.6 us
    gather x2, local copies, waits for them, and re-layouts, per_tile(): window[jnp.concatenate([local_ids, global_slots])]  22.5 us
    all_gather x1, blocking collectives, local(): seq_lists = lax.all_gather(kv_list, 'seq', axis=0, tiled=True)  22.4 us
  transfers between devices with their start and end apart: 8, of which 6 were waited for; matrix products, arithmetic and copies ran while one was open for 32% of the time, Pallas kernels for 0%

commit v1 on v0

--- a/solution.py
+++ b/solution.py
@@ -91,7 +91,9 @@
         mine = tile_id // tile_count == dev_at
         rows = lax.dynamic_slice_in_dim(stream, tile_id % tile_count * TILE, TILE, 0)
         global_rows.append(jnp.where(mine, rows, jnp.zeros_like(rows)))
-    global_stream = lax.psum(jnp.concatenate(global_rows, axis=0), ("seq", "fsdp"))
+    global_stream = jnp.sum(
+        lax.all_gather(jnp.concatenate(global_rows, axis=0), ("seq", "fsdp")), axis=0
+    )
     w_full = lax.all_gather(w_qkv, "fsdp", axis=0, tiled=True)
     normed = layer_norm(stream, ln_gain, ln_bias)
     qkv = jnp.dot(normed, w_full, preferred_element_type=jnp.float32).astype(jnp.bfloat16)

time: 550 us -> 610 us (1.11)
  other arithmetic: 19.5 us -> 45.8 us
  waiting for transfers between devices: 299 us -> 325 us
  local copies, waits for them, and re-layouts: 115 us -> 122 us
    all_gather x0 -> x1, waiting for transfers between devices: none -> 167 us  [local(): lax.all_gather(jnp.concatenate(global_rows, axis=0), ('seq', 'fsdp'))]
    psum x1 -> x0, waiting for transfers between devices: 137 us -> none  [local(): lax.psum(jnp.concatenate(global_rows, axis=0), ('seq', 'fsdp'))]
    reduce_sum x0 -> x1, other arithmetic: none -> 27.5 us  [local(): jnp.sum(lax.all_gather(jnp.concatenate(global_rows, axis=0), ('seq', 'fsd...]
    unnamed x29 -> x23, local copies, waits for them, and re-layouts: 11.8 us -> 17.1 us
  transfers between devices with their start and end apart: 8 -> 8, of which waited for: 6 -> 6; matrix products, arithmetic and copies ran while one was open for 32% -> 36% of each run, Pallas kernels for 0% -> 0%
where the time goes in v1:
time: 610 us; the launch traced here: 607 us
  waiting for transfers between devices  325 us (53%)
  local copies, waits for them, and re-layouts  122 us (20%)
  matrix products  61.2 us (10%)
  other arithmetic  45.8 us (8%)
  blocking collectives  22.3 us (4%)
  between operations  18.7 us (3%)
  starting transfers between devices  11.5 us (2%)
    all_gather x1, waiting for transfers between devices, local(): lax.all_gather(jnp.concatenate(global_rows, axis=0), ('seq', 'fsdp'))  167 us
    all_gather x1, waiting for transfers between devices, local(): w_full = lax.all_gather(w_qkv, 'fsdp', axis=0, tiled=True)  93.7 us
    ppermute x4, waiting for transfers between devices, passed_along(): return lax.ppermute(block, axis, route)  46.9 us
    while x4, local copies, waits for them, and re-layouts  35.5 us
    reduce_sum x1, other arithmetic, local(): jnp.sum(lax.all_gather(jnp.concatenate(global_rows, axis=0), ('seq', 'fsd...  27.5 us
    dot_general x2, matrix products, attend_tile(): jnp.einsum('hqk,khd->qhd', probs, values_h, preferred_element_type=jnp.fl...  23.1 us
    sub x2, matrix products, attend_tile(): weights_raw = jnp.exp(scores - row_max)  22.6 us
    gather x2, local copies, waits for them, and re-layouts, per_tile(): window[jnp.concatenate([local_ids, global_slots])]  22.5 us
  transfers between devices with their start and end apart: 8, of which 6 were waited for; matrix products, arithmetic and copies ran while one was open for 36% of the time, Pallas kernels for 0%

profile of v1, /device:TPU:28, one launch (start us, length us, event | category | flops | bytes accessed | tf_op | source)
XLA Modules:
  0.0 606.9 jit_solution(290512045069562858)
XLA Ops:
  6.5 0.7 all-gather.7.cloned.1.call-update
  7.3 0.7 convert_element_type.183
  8.1 0.7 convert_element_type.184
  8.8 0.7 compare_select_fusion.2
  9.5 1.2 gather_fusion.3
  10.7 1.3 gather_fusion.2
  12.0 0.4 convert_reduce_fusion.1
  12.4 0.3 fusion.28
  12.7 93.7 %all-gather.7.cloned.1.call-done = bf16[1280,3840]{1,0:T(8,128)(2,1)} async-done(((bf16[320,3840]{1,0:T(8,128)(2,1)}), bf16[1280,3840]{1,0:T(8,128)(2,1)}) %all-gather.7.cloned.1.call-update) | async-done | bytes 9830416 | tf_op jit(solution)/shard_map/all_gather | solution.py:97
  106.4 6.6 %convolution_convert_fusion = bf16[256,3840]{1,0:T(8,128)(2,1)S(1)} fusion(bf16[1280,3840]{1,0:T(8,128)(2,1)} %all-gather.7.cloned.1.call-done, bf16[256,1280]{1,0:T(8,128)(2,1)S(1)} %get-tuple-element.114, f32[1280]{0:T(1024)S(1)} %convert_element_type.184, f32[1280]{0:T(1024)S(1)} %convert_element_type.183, f32[256]{0:T(256)S(1)} %add_rsqrt_fusion.1, ...), kind=kOutput, calls=%fused_computation.34 | convolution fusion | flops 2519531520 | bytes 12464128 | tf_op jit(solution)/shard_map/dot_general | solution.py:99
  113.1 1.3 slice.46
  114.4 0.6 fusion.80
  120.3 0.9 pad_maximum_fusion
  121.3 0.5 all-gather.11.cloned.1.call-update
  122.0 0.2 compare_reduce_fusion.7
  122.4 22.3 %all-gather.1 = s32[32,2,16]{2,1,0:T(2,128)S(1)} all-gather(s32[1,2,16]{2,1,0:T(2,128)S(1)} %bitcast.180), channel_id=1, replica_groups=mesh['seq'=32,'fsdp'=4] {'seq'}, dimensions={0}, use_global_device_ids=true | all-gather | bytes 4224 | tf_op jit(solution)/shard_map/all_gather | solution.py:111
  145.1 0.2 compare_reduce_fusion
  146.1 0.7 fusion.65
  146.8 0.7 fusion.71
  147.5 0.7 fusion.68
  148.2 0.7 fusion.74
  148.9 3.8 fusion.61
  152.7 3.9 fusion.63
  156.6 16.0 %all-gather.9.cloned.1.call-done = bf16[1024,2560]{1,0:T(8,128)(2,1)} async-done(((bf16[256,2560]{1,0:T(8,128)(2,1)}), bf16[1024,2560]{1,0:T(8,128)(2,1)}) %all-gather.9.cloned.1.call-update) | async-done | bytes 5242896 | tf_op jit(solution)/shard_map/all_gather | solution.py:108
  172.6 4.5 gather_fusion.4
  177.1 3.0 collective-permute-start
  180.5 4.5 gather_fusion.5
  185.0 1.9 collective-permute-start.1
  187.0 4.8 gather_fusion.6
  191.7 3.4 collective-permute-start.2
  195.4 4.6 gather_fusion.7
  200.1 3.0 collective-permute-start.3
  203.1 0.8 gather_fusion.1
  204.0 5.2 constant_dynamic-update-slice_fusion.6
  209.1 22.9 %collective-permute-done = bf16[3,128,2560]{2,1,0:T(8,128)(2,1)} collective-permute-done((bf16[3,128,2560]{2,1,0:T(8,128)(2,1)}, bf16[3,128,2560]{2,1,0:T(8,128)(2,1)}, u32[]{:S(2)}, u32[]{:S(2)}) %collective-permute-start) | collective-permute-done | bytes 1966112 | tf_op jit(solution)/shard_map/ppermute | solution.py:18
  232.0 3.0 constant_dynamic-update-slice_fusion.5
  235.0 16.8 %collective-permute-done.1 = bf16[3,128,2560]{2,1,0:T(8,128)(2,1)} collective-permute-done((bf16[3,128,2560]{2,1,0:T(8,128)(2,1)}, bf16[3,128,2560]{2,1,0:T(8,128)(2,1)}, u32[]{:S(2)}, u32[]{:S(2)}) %collective-permute-start.1) | collective-permute-done | bytes 1966112 | tf_op jit(solution)/shard_map/ppermute | solution.py:18
  251.8 3.0 constant_dynamic-update-slice_fusion.4
  254.8 2.9 constant_dynamic-update-slice_fusion.3
  257.7 7.2 %collective-permute-done.3 = bf16[3,128,2560]{2,1,0:T(8,128)(2,1)} collective-permute-done((bf16[3,128,2560]{2,1,0:T(8,128)(2,1)}, bf16[3,128,2560]{2,1,0:T(8,128)(2,1)}, u32[]{:S(2)}, u32[]{:S(2)}) %collective-permute-start.3) | collective-permute-done | bytes 1966112 | tf_op jit(solution)/shard_map/ppermute | solution.py:18
  264.9 3.0 constant_dynamic-update-slice_fusion.2
  267.9 167.1 %all-gather.13.cloned.1.call-done = bf16[32768,1280]{1,0:T(8,128)(2,1)} async-done(((bf16[256,1280]{1,0:T(8,128)(2,1)}), bf16[32768,1280]{1,0:T(8,128)(2,1)}) %all-gather.13.cloned.1.call-update) | async-done | bytes 83886096 | tf_op jit(solution)/shard_map/all_gather | solution.py:95
  435.0 27.5 %reduce_sum.179 = bf16[256,1280]{1,0:T(8,128)(2,1)S(1)} reduce(bf16[128,256,1280]{2,1,0:T(8,128)(2,1)} %bitcast.41, bf16[]{:T(256)} %constant.158.clone.1), dimensions={0}, to_apply=%region_30.31 | reduce | flops 41615360 | bytes 84541440 | tf_op jit(solution)/shard_map/reduce_sum | solution.py:94
  462.7 0.3 fusion.24
  463.1 5.0 fusion.17
  468.1 1.2 constant_dynamic-update-slice_fusion.1
  469.3 127.2 %while.11 = (s32[]{:T(128)}, bf16[2,128,1280]{2,1,0:T(8,128)(2,1)S(1)}, s32[2,16]{1,0:T(2,128)S(1)}, bf16[22,128,2560]{2,1,0:T(8,128)(2,1)}, s32[2]{0:T(128)S(1)...) while((s32[]{:T(128)}, bf16[2,128,1280]{2,1,0:T(8,128)(2,1)S(1)}, ...), condition=%wide.region_36.37_spmd.clone, body=%wide.region_33.36_spmd.clone.sunk | while | flops 1538428160 | bytes 123626600 | solution.py:148
  469.3 0.6 dynamic_slice.54
  469.8 0.6 iota_compare_fusion.2
  470.9 11.3 %gather_fusion = bf16[18,128,2560]{2,1,0:T(8,128)(2,1)} fusion(bf16[22,128,2560]{2,1,0:T(8,128)(2,1)} %get-tuple-element.205, s32[1024]{0:T(1024)S(1)} %pad_clamp_fusion.8), kind=kCustom, calls=%fused_computation.clone.clone.1 | custom fusion | bytes 23593032 | tf_op jit(solution)/shard_map/while/body/eval_jaxpr/gather | solution.py:143
  482.2 9.8 %fusion.102 = (bf16[2304,1280]{1,0:T(8,128)(2,1)}, bf16[2304,1280]{1,0:T(8,128)(2,1)}) fusion(bf16[2304,2560]{1,0:T(8,128)(2,1)} %bitcast.167), kind=kLoop, calls=%fused_computation.186.clone.1 | loop fusion | bytes 23592960 | tf_op jit(solution)/shard_map/while/body/eval_jaxpr/slice | solution.py:53
  492.0 8.9 %copy.37 = bf16[2304,1280]{0,1:T(8,128)(2,1)} copy(bf16[2304,1280]{1,0:T(8,128)(2,1)} %get-tuple-element.182) | data formatting | bytes 11796480 | tf_op jit(solution)/shard_map/while
  500.9 8.9 %copy.39 = bf16[2304,1280]{0,1:T(8,128)(2,1)} copy(bf16[2304,1280]{1,0:T(8,128)(2,1)} %get-tuple-element.183) | data formatting | bytes 11796480 | tf_op jit(solution)/shard_map/while
  509.8 11.3 %fusion.103 = (f32[16,128]{1,0:T(8,128)S(1)}, f32[16,128,2304]{2,1,0:T(8,128)}) fusion(pred[2304]{0:T(1024)(128)(4,1)S(1)} %broadcast_bitcast_fusion.2, bf16[128,16,80]{0,2,1:T(8,128)(2,1)S(1)} %bitcast.175, bf16[2304,16,80]{0,2,1:T(8,128)(2,1)} %bitcast.169), kind=kOutput, calls=%fused_computation.187.clone.1 | convolution fusion | flops 773851392 | bytes 25110784 | tf_op jit(solution)/shard_map/while/body/eval_jaxpr/sub | solution.py:60
  521.1 11.5 %fusion.104 = bf16[16,80,128]{2,1,0:T(8,128)(2,1)S(1)} fusion(bf16[2304,16,80]{0,2,1:T(8,128)(2,1)} %bitcast.168, f32[16,128,2304]{2,1,0:T(8,128)} %get-tuple-element.184, f32[16,128]{1,0:T(8,128)S(1)} %get-tuple-element.185), kind=kOutput, calls=%fused_computation.19.clone.1 | convolution fusion | flops 764575744 | bytes 25108480 | tf_op jit(solution)/shard_map/while/body/eval_jaxpr/hqk,khd->qhd/dot_general | solution.py:62
  532.9 0.6 dynamic_slice.54
  533.5 0.6 iota_compare_fusion.2
  534.6 11.3 %gather_fusion = bf16[18,128,2560]{2,1,0:T(8,128)(2,1)} fusion(bf16[22,128,2560]{2,1,0:T(8,128)(2,1)} %get-tuple-element.205, s32[1024]{0:T(1024)S(1)} %pad_clamp_fusion.8), kind=kCustom, calls=%fused_computation.clone.clone.1 | custom fusion | bytes 23593032 | tf_op jit(solution)/shard_map/while/body/eval_jaxpr/gather | solution.py:143
  545.8 9.8 %fusion.102 = (bf16[2304,1280]{1,0:T(8,128)(2,1)}, bf16[2304,1280]{1,0:T(8,128)(2,1)}) fusion(bf16[2304,2560]{1,0:T(8,128)(2,1)} %bitcast.167), kind=kLoop, calls=%fused_computation.186.clone.1 | loop fusion | bytes 23592960 | tf_op jit(solution)/shard_map/while/body/eval_jaxpr/slice | solution.py:53
  555.6 8.9 %copy.37 = bf16[2304,1280]{0,1:T(8,128)(2,1)} copy(bf16[2304,1280]{1,0:T(8,128)(2,1)} %get-tuple-element.182) | data formatting | bytes 11796480 | tf_op jit(solution)/shard_map/while
  564.5 8.9 %copy.39 = bf16[2304,1280]{0,1:T(8,128)(2,1)} copy(bf16[2304,1280]{1,0:T(8,128)(2,1)} %get-tuple-element.183) | data formatting | bytes 11796480 | tf_op jit(solution)/shard_map/while
  573.4 11.3 %fusion.103 = (f32[16,128]{1,0:T(8,128)S(1)}, f32[16,128,2304]{2,1,0:T(8,128)}) fusion(pred[2304]{0:T(1024)(128)(4,1)S(1)} %broadcast_bitcast_fusion.2, bf16[128,16,80]{0,2,1:T(8,128)(2,1)S(1)} %bitcast.175, bf16[2304,16,80]{0,2,1:T(8,128)(2,1)} %bitcast.169), kind=kOutput, calls=%fused_computation.187.clone.1 | convolution fusion | flops 773851392 | bytes 25110784 | tf_op jit(solution)/shard_map/while/body/eval_jaxpr/sub | solution.py:60
  584.7 11.6 %fusion.104 = bf16[16,80,128]{2,1,0:T(8,128)(2,1)S(1)} fusion(bf16[2304,16,80]{0,2,1:T(8,128)(2,1)} %bitcast.168, f32[16,128,2304]{2,1,0:T(8,128)} %get-tuple-element.184, f32[16,128]{1,0:T(8,128)S(1)} %get-tuple-element.185), kind=kOutput, calls=%fused_computation.19.clone.1 | convolution fusion | flops 764575744 | bytes 25108480 | tf_op jit(solution)/shard_map/while/body/eval_jaxpr/hqk,khd->qhd/dot_general | solution.py:62
  596.5 3.9 convolution_convert_fusion.1
  (94 shorter events, 4.0 us)
Async XLA Ops:
  6.5 2.9 copy-start
  6.5 99.9 %all-gather.7.cloned.1.call-start = ((), (), s32[]{:S(2)}) async-start(), calls=%async_computation | async-start | bytes 12288000 | tf_op jit(solution)/shard_map/all_gather | solution.py:97
  7.3 3.5 copy-start.2
  7.3 165.4 %all-gather.9.cloned.1.call-start = ((), (), s32[]{:S(2)}) async-start(), calls=%async_computation.1 | async-start | bytes 6553600 | tf_op jit(solution)/shard_map/all_gather | solution.py:108
  10.7 1.3 copy-start.4
  113.1 90.9 %copy-start.3 = (bf16[256,3840]{1,0:T(8,128)(2,1)}, bf16[256,3840]{1,0:T(8,128)(2,1)S(1)}, u32[]{:S(2)}) copy-start(bf16[256,3840]{1,0:T(8,128)(2,1)S(1)} %convolution_convert_fusion) | copy-start | bytes 5898244
  113.1 1.4 copy-start.6
  114.3 7.6 %copy-start.5 = (s32[2,16]{1,0:T(2,128)S(1)}, s32[2,16]{1,0:T(2,128)}, u32[]{:S(2)}) copy-start(s32[2,16]{1,0:T(2,128)} %param.15) | copy-start | bytes 388
  114.4 320.7 %all-gather.13.cloned.1.call-start = ((), (), s32[]{:S(2)}) async-start(), calls=%async_computation.3 | async-start | bytes 84541440 | tf_op jit(solution)/shard_map/all_gather | solution.py:95
  121.2 475.3 %all-gather.11.cloned.1.call-start = ((), (), s32[]{:S(2)}) async-start(), calls=%async_computation.2 | async-start | bytes 4096000 | tf_op jit(solution)/shard_map/all_gather | solution.py:153
  177.1 54.9 %collective-permute-start = (bf16[3,128,2560]{2,1,0:T(8,128)(2,1)}, bf16[3,128,2560]{2,1,0:T(8,128)(2,1)}, u32[]{:S(2)}, u32[]{:S(2)}) collective-permute-start(bf16[3,128,2560]{2,1,0:T(8,128)(2,1)} %gather_fusion.4), channel_id=1, source_target_pairs={{0,8},{4,12},{8,16},{12,20},{16,24},{20,28},{24,32},{28,36},{32,40... | collective-permute-start | bytes 5898248 | tf_op jit(solution)/shard_map/ppermute | solution.py:18
  185.0 66.7 %collective-permute-start.1 = (bf16[3,128,2560]{2,1,0:T(8,128)(2,1)}, bf16[3,128,2560]{2,1,0:T(8,128)(2,1)}, u32[]{:S(2)}, u32[]{:S(2)}) collective-permute-start(bf16[3,128,2560]{2,1,0:T(8,128)(2,1)} %gather_fusion.5), channel_id=1, source_target_pairs={{0,4},{4,8},{8,12},{12,16},{16,20},{20,24},{24,28},{28,32},{32,36}... | collective-permute-start | bytes 5898248 | tf_op jit(solution)/shard_map/ppermute | solution.py:18
  191.7 63.1 %collective-permute-start.2 = (bf16[3,128,2560]{2,1,0:T(8,128)(2,1)}, bf16[3,128,2560]{2,1,0:T(8,128)(2,1)}, u32[]{:S(2)}, u32[]{:S(2)}) collective-permute-start(bf16[3,128,2560]{2,1,0:T(8,128)(2,1)} %gather_fusion.6), channel_id=1, source_target_pairs={{4,0},{8,4},{12,8},{16,12},{20,16},{24,20},{28,24},{32,28},{36,32}... | collective-permute-start | bytes 5898248 | tf_op jit(solution)/shard_map/ppermute | solution.py:18
  200.1 64.9 %collective-permute-start.3 = (bf16[3,128,2560]{2,1,0:T(8,128)(2,1)}, bf16[3,128,2560]{2,1,0:T(8,128)(2,1)}, u32[]{:S(2)}, u32[]{:S(2)}) collective-permute-start(bf16[3,128,2560]{2,1,0:T(8,128)(2,1)} %gather_fusion.7), channel_id=1, source_target_pairs={{8,0},{12,4},{16,8},{20,12},{24,16},{28,20},{32,24},{36,28},{40,32... | collective-permute-start | bytes 5898248 | tf_op jit(solution)/shard_map/ppermute | solution.py:18
  463.0 6.2 %slice-start = ((bf16[256,3840]{1,0:T(8,128)(2,1)}), bf16[256,1280]{1,0:T(8,128)(2,1)S(1)}, s32[]{:S(2)}) async-start(bf16[256,3840]{1,0:T(8,128)(2,1)} %copy-done.3), calls=%async_computation.4 | async-start | bytes 1310720 | tf_op jit(solution)/shard_map/slice | solution.py:100
  463.0 6.2 %copy-start.7 = (bf16[2,128,1280]{2,1,0:T(8,128)(2,1)S(1)}, bf16[2,128,1280]{2,1,0:T(8,128)(2,1)}, u32[]{:S(2)}) copy-start(bf16[2,128,1280]{2,1,0:T(8,128)(2,1)} %custom-call.17) | copy-start | bytes 1966084
  463.0 6.2 %copy-start.8 = (s32[2]{0:T(128)S(1)}, s32[2]{0:T(128)}, u32[]{:S(2)}) copy-start(s32[2]{0:T(128)} %param.16) | copy-start | bytes 28
  596.5 3.9 copy-start.1
Sparse Core Ops, SparseCore 0:
  9.0 97.3 all-gather.6
  114.5 58.1 all-gather.8
  175.6 259.3 all-gather.12
  436.5 39.7 all-gather.10
